TPU v7x, 512 devices: a whole 4x4x16 slice. The times are simulated.
512 devices in a mesh: mpo: 16 (over z), sec: 32 (over x, y, core).
Axes of the slice: x: 4, y: 4, z: 16, core: 2. Of those that a mesh axis runs over, the one named last changes fastest.
Arguments:
- environment: bfloat16 [48, 64, 128, 128], P('mpo', 'sec'), may hold values from -6 to 6
- site_tensor: bfloat16 [64, 4, 128, 128], P('sec'), may hold values from -0.25 to 0.25
- mpo_tensor: bfloat16 [48, 48, 4, 4], P('mpo'), may hold values from -0.75 to 0.75
- mpo_pattern: int32 [48, 48], P('mpo'), may hold values 0 or 1
- sector_rows: int32 [64], replicated, may hold values from 64 to 128
- sector_map: int32 [64], replicated, may hold values from 0 to 63, as said below
Outputs:
- new_environment: bfloat16 [48, 64, 128, 128], P('mpo', 'sec')
Inputs may be any that keep to these rules, and one draw needn't show every extreme that they name: A permutation of the 64 sector labels: sector g takes the new label sector_map[g].
All inputs are finite; a program needn't handle non-finite values. No bound on the sum of `mpo_pattern` on one device may be relied on, other than what follows from the above.
Results may differ from a plain program's by a relative error of at most 0.02.
Values may be sent and summed in bfloat16 or wider, within the bound.
No kernel may reach another device: no remote copies, remote signals or barrier semaphores. Data moves between devices by JAX's collectives and lax.ppermute only.
A program may use at most 64 MiB of HBM per device.

v0:
```python
import jax
import jax.numpy as jnp
from jax import lax
from jax.sharding import PartitionSpec as P


def per_device(environment, site_tensor, mpo_tensor, mpo_pattern, sector_rows, sector_map):
    per_dev = environment.shape[1]
    block = environment.shape[2]
    masked = jnp.where(mpo_pattern[:, :, None, None] != 0, mpo_tensor, jnp.zeros_like(mpo_tensor))
    left = jnp.einsum(
        "gsxa,bgxc->gbsac", site_tensor, environment, preferred_element_type=jnp.float32
    ).astype(jnp.bfloat16)
    sandwich = jnp.einsum(
        "gbsac,gtcz->bstgaz", left, site_tensor, preferred_element_type=jnp.float32
    ).astype(jnp.bfloat16)
    parts = jnp.einsum(
        "bpst,bstgaz->pgaz", masked, sandwich, preferred_element_type=jnp.float32
    ).astype(jnp.bfloat16)
    summed = lax.psum_scatter(parts, "mpo", scatter_dimension=0, tiled=True)
    device = lax.axis_index("sec")
    local = jnp.arange(per_dev, dtype=jnp.int32)
    own_labels = device * per_dev + local
    sizes = jnp.take(sector_rows, own_labels, axis=0)
    places = jnp.arange(block, dtype=jnp.int32)
    keep = (places[None, :, None] < sizes[:, None, None]) & (
        places[None, None, :] < sizes[:, None, None]
    )
    result = jnp.where(keep[None, :, :, :], summed, jnp.zeros_like(summed))
    gathered = lax.all_gather(result, "sec", axis=1, tiled=True)
    nsec = sector_map.shape[0]
    inverse = jnp.zeros((nsec,), jnp.int32).at[sector_map].set(jnp.arange(nsec, dtype=jnp.int32))
    source = jnp.take(inverse, own_labels, axis=0)
    return jnp.take(gathered, source, axis=1)


def solution(mesh):
    return jax.shard_map(
        per_device,
        mesh=mesh,
        in_specs=(
            P("mpo", "sec", None, None),
            P("sec", None, None, None),
            P("mpo", None, None, None),
            P("mpo", None),
            P(),
            P(),
        ),
        out_specs=P("mpo", "sec", None, None),
        check_vma=False,
    )
```

profile of v0, /device:TPU:1, one launch (start us, length us, event | category | flops | bytes accessed | tf_op | source)
XLA Modules:
  0.0 175.2 jit_solution(12927616610973831131)
XLA Ops:
  6.5 0.0 copy-start
  6.5 0.0 copy-start.2
  6.5 0.0 reduce-scatter.2.cloned.1.call-start
  6.5 0.7 broadcast_compare_fusion
  7.3 0.2 copy-done
  7.5 2.1 %convert_bitcast_fusion = bf16[3,4,4,2,128,128]{5,4,2,1,0,3:T(8,128)(2,1)S(1)} fusion(bf16[2,4,128,128]{3,2,1,0:T(8,128)(2,1)S(1)} %copy-done, bf16[3,2,128,128]{3,2,1,0:T(8,128)(2,1)} %param.8), kind=kOutput, calls=%fused_computation.7 | convolution fusion | flops 505282560 | bytes 3604480 | tf_op jit(solution)/shard_map/gbsac,gtcz->bstgaz/dot_general | solution.py:14
  9.7 0.0 copy-done.2
  9.7 4.0 %bitcast_convert_fusion = bf16[48,2,128,128]{3,0,2,1:T(8,128)(2,1)S(1)} fusion(bf16[3,4,4,2,128,128]{5,4,2,1,0,3:T(8,128)(2,1)S(1)} %convert_bitcast_fusion, bf16[3,48,4,4]{1,3,2,0:T(4,128)(2,1)S(1)} %copy-done.2, pred[3,48]{1,0:T(4,128)(4,1)S(1)} %broadcast_compare_fusion), kind=kOutput, calls=%fused_computation.4 | convolution fusion | flops 152570112 | bytes 6296208 | tf_op jit(solution)/shard_map/bpst,bstgaz->pgaz/dot_general | solution.py:17
  13.7 2.5 %copy.12 = bf16[48,2,128,128]{3,2,1,0:T(8,128)(2,1)} copy(bf16[48,2,128,128]{3,0,2,1:T(8,128)(2,1)S(1)} %bitcast_convert_fusion) | data formatting | bytes 6291456 | tf_op jit(solution)/shard_map/convert_element_type | solution.py:19
  16.2 0.0 copy-start.1
  16.2 0.0 copy-start.3
  16.2 0.0 reduce-scatter.2.cloned.1.call-update
  16.2 0.0 all-gather.2.cloned.1.call-start
  16.3 0.5 copy-done.1
  16.8 0.6 gather_fusion.2
  17.5 0.1 iota_compare_fusion
  17.6 0.1 broadcast_and_fusion
  17.7 71.9 %reduce-scatter.2.cloned.1.call-done = bf16[3,2,128,128]{3,2,1,0:T(8,128)(2,1)} async-done(((bf16[48,2,128,128]{3,2,1,0:T(8,128)(2,1)}), bf16[3,2,128,128]{3,2,1,0:T(8,128)(2,1)}) %reduce-scatter.2.cloned.1.call-update) | async-done | bytes 196624 | tf_op jit(solution)/shard_map/reduce_scatter | solution.py:20
  89.6 0.9 broadcast_select_fusion
  90.5 0.7 copy.13
  91.2 0.0 all-gather.2.cloned.1.call-update
  91.3 0.0 copy-done.3
  91.3 0.8 scatter_custom_fusion
  92.1 0.6 gather_fusion.1
  92.7 71.5 %all-gather.2.cloned.1.call-done = bf16[3,64,128,128]{3,2,0,1:T(8,128)(2,1)} async-done(((bf16[3,2,128,128]{3,2,0,1:T(8,128)(2,1)}), bf16[3,64,128,128]{3,2,0,1:T(8,128)(2,1)}) %all-gather.2.cloned.1.call-update) | async-done | bytes 6291472 | tf_op jit(solution)/shard_map/all_gather | solution.py:30
  164.2 3.4 %gather_fusion = bf16[2,3,128,128]{3,2,1,0:T(8,128)(2,1)S(1)} fusion(bf16[3,64,128,128]{3,2,0,1:T(8,128)(2,1)} %all-gather.2.cloned.1.call-done, s32[1024]{0:T(1024)S(1)} %pad_clamp_fusion), kind=kCustom, calls=%fused_computation.2 | custom fusion | bytes 393224 | tf_op jit(solution)/shard_map/jit(_take)/gather | solution.py:34
  167.6 0.1 select_bitcast_fusion
  167.7 0.7 copy.14
  (7 shorter events, 0.0 us)
Async XLA Ops:
  6.5 1.0 copy-start
  6.5 3.1 %copy-start.2 = (bf16[3,48,4,4]{1,3,2,0:T(4,128)(2,1)S(1)}, bf16[3,48,4,4]{1,3,2,0:T(4,128)(2,1)}, u32[]{:S(2)}) copy-start(bf16[3,48,4,4]{1,3,2,0:T(4,128)(2,1)} %param.10) | copy-start | bytes 13828
  6.5 83.1 %reduce-scatter.2.cloned.1.call-start = ((), (), s32[]{:S(2)}) async-start(), calls=%async_computation.1 | async-start | bytes 3342336 | tf_op jit(solution)/shard_map/reduce_scatter | solution.py:20
  16.2 0.7 copy-start.1
  16.2 75.1 %copy-start.3 = (s32[64]{0:T(128)S(1)}, s32[64]{0:T(128)}, u32[]{:S(2)}) copy-start(s32[64]{0:T(128)} %param.13) | copy-start | bytes 772
  16.2 148.0 %all-gather.2.cloned.1.call-start = ((), (), s32[]{:S(2)}) async-start(), calls=%async_computation.2 | async-start | bytes 6488064 | tf_op jit(solution)/shard_map/all_gather | solution.py:30
Sparse Core Ops, SparseCore 0:
  16.3 73.2 reduce-scatter.1
  92.7 71.4 all-gather.1
where the time goes:
time: 175 us
  waiting for transfers between devices  143 us (82%)
  between operations  13.5 us (8%)
  local copies, waits for them, and re-layouts  10.1 us (6%)
  matrix products  6.18 us (4%)
  other arithmetic  1.98 us (1%)
    reduce_scatter x1, waiting for transfers between devices, per_device(): summed = lax.psum_scatter(parts, 'mpo', scatter_dimension=0, tiled=True)  71.9 us
    all_gather x1, waiting for transfers between devices, per_device(): gathered = lax.all_gather(result, 'sec', axis=1, tiled=True)  71.5 us
    dot_general x1, matrix products, per_device(): jnp.einsum('bpst,bstgaz->pgaz', masked, sandwich, preferred_element_type=...  4.03 us
  transfers between devices with their start and end apart: 2, of which 2 were waited for; matrix products, arithmetic and copies ran while one was open for 1% of the time, Pallas kernels for 0%

commit v1 on v0

--- a/solution.py
+++ b/solution.py
@@ -2,6 +2,10 @@
 import jax.numpy as jnp
 from jax import lax
 from jax.sharding import PartitionSpec as P
+
+_answer_spans = lambda work_x, axis_name: jnp.concatenate(
+    lax.all_to_all(jnp.stack([work_x] * lax.axis_size(axis_name), axis=0), axis_name, 0, 0), axis=1
+)
 
 
 def per_device(environment, site_tensor, mpo_tensor, mpo_pattern, sector_rows, sector_map):
@@ -27,7 +31,7 @@
         places[None, None, :] < sizes[:, None, None]
     )
     result = jnp.where(keep[None, :, :, :], summed, jnp.zeros_like(summed))
-    gathered = lax.all_gather(result, "sec", axis=1, tiled=True)
+    gathered = _answer_spans(result, "sec")
     nsec = sector_map.shape[0]
     inverse = jnp.zeros((nsec,), jnp.int32).at[sector_map].set(jnp.arange(nsec, dtype=jnp.int32))
     source = jnp.take(inverse, own_labels, axis=0)

time: 175 us -> 218 us (1.25)
  the two profiles are of different devices: /device:TPU:1 before, /device:TPU:8 now
where the time goes in v1:
time: 218 us
  waiting for transfers between devices  167 us (77%)
  local copies, waits for them, and re-layouts  21.7 us (10%)
  between operations  13.5 us (6%)
  starting transfers between devices  7.74 us (4%)
  matrix products  6.18 us (3%)
    all_to_all x1, waiting for transfers between devices, lax.all_to_all(jnp.stack([work_x] * lax.axis_size(axis_name), axis=0), ax...  87 us
    reduce_scatter x1, waiting for transfers between devices, per_device(): summed = lax.psum_scatter(parts, 'mpo', scatter_dimension=0, tiled=True)  79.9 us
    all_to_all x1, local copies, waits for them, and re-layouts, lax.all_to_all(jnp.stack([work_x] * lax.axis_size(axis_name), axis=0), ax...  8.07 us
    all_to_all x1, starting transfers between devices, lax.all_to_all(jnp.stack([work_x] * lax.axis_size(axis_name), axis=0), ax...  7.74 us
  transfers between devices with their start and end apart: 2, of which 2 were waited for; matrix products, arithmetic and copies ran while one was open for 1% of the time, Pallas kernels for 0%

profile of v1, /device:TPU:8, one launch (start us, length us, event | category | flops | bytes accessed | tf_op | source)
XLA Modules:
  0.0 218.0 jit_solution(9052111344644544600)
XLA Ops:
  6.5 0.0 copy-start
  6.5 0.0 copy-start.2
  6.5 0.0 reduce-scatter.2.cloned.1.call-start
  6.5 0.7 broadcast_compare_fusion
  7.3 0.2 copy-done
  7.5 2.1 convert_bitcast_fusion
  9.7 0.0 copy-done.2
  9.7 4.0 %bitcast_convert_fusion = bf16[48,2,128,128]{3,0,2,1:T(8,128)(2,1)S(1)} fusion(bf16[3,4,4,2,128,128]{5,4,2,1,0,3:T(8,128)(2,1)S(1)} %convert_bitcast_fusion, bf16[3,48,4,4]{1,3,2,0:T(4,128)(2,1)S(1)} %copy-done.2, pred[3,48]{1,0:T(4,128)(4,1)S(1)} %broadcast_compare_fusion), kind=kOutput, calls=%fused_computation.4 | convolution fusion | flops 152570112 | bytes 6296208 | tf_op jit(solution)/shard_map/bpst,bstgaz->pgaz/dot_general | solution.py:21
  13.7 2.5 %copy.13 = bf16[48,2,128,128]{3,2,1,0:T(8,128)(2,1)} copy(bf16[48,2,128,128]{3,0,2,1:T(8,128)(2,1)S(1)} %bitcast_convert_fusion) | data formatting | bytes 6291456 | tf_op jit(solution)/shard_map/convert_element_type | solution.py:23
  16.2 0.0 copy-start.1
  16.2 0.0 reduce-scatter.2.cloned.1.call-update
  16.2 0.6 copy-done.1
  16.8 0.6 gather_fusion.2
  17.5 0.1 iota_compare_fusion
  17.6 0.1 broadcast_and_fusion
  17.7 79.9 %reduce-scatter.2.cloned.1.call-done = bf16[3,2,128,128]{3,2,1,0:T(8,128)(2,1)} async-done(((bf16[48,2,128,128]{3,2,1,0:T(8,128)(2,1)}), bf16[3,2,128,128]{3,2,1,0:T(8,128)(2,1)}) %reduce-scatter.2.cloned.1.call-update) | async-done | bytes 196624 | tf_op jit(solution)/shard_map/reduce_scatter | solution.py:24
  97.5 0.9 broadcast_select_fusion
  98.5 4.2 %stack.2 = bf16[32,3,2,128,128]{4,3,2,1,0:T(8,128)(2,1)} broadcast(bf16[3,2,128,128]{3,2,1,0:T(8,128)(2,1)S(1)} %broadcast_select_fusion), dimensions={1,2,3,4} | broadcast | bytes 6488064 | tf_op jit(solution)/shard_map/stack | solution.py:7
  102.7 0.0 copy-start.3
  102.7 7.7 %all-to-all-start = ((bf16[32,3,2,128,128]{4,3,2,1,0:T(8,128)(2,1)}), bf16[32,3,2,128,128]{4,3,2,1,0:T(8,128)(2,1)}, u32[]{:S(2)}, u32[]{:S(2)}) async-start(bf16[32,3,2,128,128]{4,3,2,1,0:T(8,128)(2,1)} %stack.2), calls=%async_computation.1 | async-start | bytes 12582912 | tf_op jit(solution)/shard_map/all_to_all | solution.py:7
  110.5 0.0 copy-done.3
  110.5 0.8 scatter_custom_fusion
  111.3 0.6 gather_fusion.1
  112.0 87.0 %all-to-all-done = bf16[32,3,2,128,128]{4,3,2,1,0:T(8,128)(2,1)} async-done(((bf16[32,3,2,128,128]{4,3,2,1,0:T(8,128)(2,1)}), bf16[32,3,2,128,128]{4,3,2,1,0:T(8,128)(2,1)}, u32[]{:S(2)}, u32[]{:S(2)}) %all-to-all-start) | async-done | bytes 6291488 | tf_op jit(solution)/shard_map/all_to_all | solution.py:7
  199.0 8.1 %copy.14 = bf16[32,3,2,128,128]{4,3,2,0,1:T(8,128)(2,1)} copy(bf16[32,3,2,128,128]{4,3,2,1,0:T(8,128)(2,1)} %all-to-all-done) | data formatting | bytes 12582912 | tf_op jit(solution)/shard_map/all_to_all | solution.py:7
  207.0 3.4 %gather_fusion = bf16[2,3,128,128]{3,2,1,0:T(8,128)(2,1)S(1)} fusion(bf16[3,64,128,128]{3,2,1,0:T(8,128)(2,1)} %bitcast.41, s32[1024]{0:T(1024)S(1)} %pad_clamp_fusion), kind=kCustom, calls=%fused_computation.2 | custom fusion | bytes 393224 | tf_op jit(solution)/shard_map/jit(_take)/gather | solution.py:38
  210.4 0.1 select_bitcast_fusion
  210.5 0.7 copy.15
  (7 shorter events, 0.0 us)
Async XLA Ops:
  6.5 1.0 copy-start
  6.5 3.1 %copy-start.2 = (bf16[3,48,4,4]{1,3,2,0:T(4,128)(2,1)S(1)}, bf16[3,48,4,4]{1,3,2,0:T(4,128)(2,1)}, u32[]{:S(2)}) copy-start(bf16[3,48,4,4]{1,3,2,0:T(4,128)(2,1)} %param.10) | copy-start | bytes 13828
  6.5 91.0 %reduce-scatter.2.cloned.1.call-start = ((), (), s32[]{:S(2)}) async-start(), calls=%async_computation.2 | async-start | bytes 3342336 | tf_op jit(solution)/shard_map/reduce_scatter | solution.py:24
  16.2 0.7 copy-start.1
  102.7 7.8 %copy-start.3 = (s32[64]{0:T(128)S(1)}, s32[64]{0:T(128)}, u32[]{:S(2)}) copy-start(s32[64]{0:T(128)} %param.13) | copy-start | bytes 772
  102.7 96.2 %all-to-all-start = ((bf16[32,3,2,128,128]{4,3,2,1,0:T(8,128)(2,1)}), bf16[32,3,2,128,128]{4,3,2,1,0:T(8,128)(2,1)}, u32[]{:S(2)}, u32[]{:S(2)}) async-start(bf16[32,3,2,128,128]{4,3,2,1,0:T(8,128)(2,1)} %stack.2), calls=%async_computation.1 | async-start | bytes 12582912 | tf_op jit(solution)/shard_map/all_to_all | solution.py:7
Sparse Core Ops, SparseCore 0:
  16.3 81.1 reduce-scatter.1
